TPU v7x, 256 devices: a whole 4x4x8 slice. The times are simulated.
256 devices in a mesh: rows: 16 (over x, y), sub: 16 (over z, core).
Axes of the slice: x: 4, y: 4, z: 8, core: 2. Of those that a mesh axis runs over, the one named last changes fastest.
Arguments:
- embeddings: bfloat16 [65536, 1024], P(('rows', 'sub'))
- codes: int32 [64, 65536], P(None, ('rows', 'sub')), may hold values from 0 to 255
- codebook: bfloat16 [256, 1024], P(None, 'sub'), may hold values from -6 to 6
Outputs:
- rotation: float32 [1024, 1024], P('sub')
- rotated: bfloat16 [65536, 1024], P(('rows', 'sub'))
- new_codebook: float32 [256, 1024], P(None, 'sub')
All inputs are finite; a program needn't handle non-finite values.
Results may differ from a plain program's by a relative error of at most 0.0095.
Values may be sent and summed in bfloat16 or wider, within the bound.
No kernel may reach another device: no remote copies, remote signals or barrier semaphores. Data moves between devices by JAX's collectives and lax.ppermute only.
A program may use at most 64 MiB of HBM per device.

v0:
```python
import math
import jax
import jax.numpy as jnp
from jax import lax
from jax.sharding import PartitionSpec as P

NS_STEPS = 3
coef_a = 3.4445
coef_b = -4.775
coef_c = 2.0315
frob_eps = 1e-07


def one_hot_codes(code_block, count_codes):
    levels = lax.broadcasted_iota(jnp.int32, code_block.shape + (count_codes,), 2)
    return (code_block[:, :, None] == levels).astype(jnp.bfloat16)


def decode_rows(codes, table):
    subspaces, local_rows = codes.shape
    count_codes, row_width = table.shape
    sub_width = row_width // subspaces
    codewords = table.reshape(count_codes, subspaces, sub_width)
    one_hot = one_hot_codes(codes, count_codes)
    picked = jnp.einsum("mnk,kmj->nmj", one_hot, codewords, preferred_element_type=jnp.float32)
    return picked.reshape(local_rows, row_width).astype(jnp.bfloat16)


def codeword_totals(codes, row_values, count_codes):
    subspaces, local_rows = codes.shape
    row_width = row_values.shape[1]
    sub_width = row_width // subspaces
    one_hot = one_hot_codes(codes, count_codes)
    pieces = row_values.reshape(local_rows, subspaces, sub_width)
    code_sums = jnp.einsum("mnk,nmj->kmj", one_hot, pieces, preferred_element_type=jnp.float32)
    counts = jnp.sum(one_hot, axis=1, dtype=jnp.float32).T
    return (code_sums.reshape(count_codes, row_width), counts)


def bdot(left, right, dims):
    return lax.dot_general(
        left.astype(jnp.bfloat16),
        right.astype(jnp.bfloat16),
        (dims, ((), ())),
        preferred_element_type=jnp.float32,
    )


def newton_step(z):
    z_half = z.astype(jnp.bfloat16)
    gram = bdot(z_half, z_half, ((1,), (1,)))
    quartic = bdot(gram, gram, ((1,), (0,)))
    mixer = coef_b * gram + coef_c * quartic
    return coef_a * z + bdot(mixer, z_half, ((1,), (0,)))


def body(embeddings, codes, codebook):
    table = lax.all_gather(codebook, "sub", axis=1, tiled=True)
    decoded = decode_rows(codes, table)
    partial = lax.dot_general(
        embeddings, decoded, (((0,), (0,)), ((), ())), preferred_element_type=jnp.float32
    )
    cross = lax.psum(partial, ("rows", "sub"))
    frob_scale = jnp.sqrt(jnp.sum(cross * cross)) + frob_eps
    z = cross / frob_scale
    for newton_step_index in range(NS_STEPS):
        z = newton_step(z)
    rotation_half = z.astype(jnp.bfloat16)
    rotated = jnp.dot(embeddings, rotation_half, preferred_element_type=jnp.float32).astype(
        jnp.bfloat16
    )
    code_sums, counts = codeword_totals(codes, rotated, table.shape[0])
    code_sums = lax.psum(code_sums, ("rows", "sub"))
    counts = lax.psum(counts, ("rows", "sub"))
    me = lax.axis_index("sub")
    cols = codebook.shape[1]
    own_subspaces = counts.shape[1] * cols // code_sums.shape[1]
    own_sums = lax.dynamic_slice_in_dim(code_sums, me * cols, cols, axis=1)
    own_counts = lax.dynamic_slice_in_dim(counts, me * own_subspaces, own_subspaces, axis=1)
    own_codebook = codebook.astype(jnp.float32)
    spread = jnp.repeat(own_counts, cols // own_subspaces, axis=1)
    new_codebook = (own_sums + own_codebook) / (spread + 1.0)
    panel_rows = z.shape[0] // lax.axis_size("sub")
    panel = lax.dynamic_slice_in_dim(z, me * panel_rows, panel_rows, axis=0)
    return (panel, rotated, new_codebook)


def solution(mesh):
    in_specs = (P(("rows", "sub"), None), P(None, ("rows", "sub")), P(None, "sub"))
    out_specs = (P("sub", None), P(("rows", "sub"), None), P(None, "sub"))
    return jax.shard_map(body, mesh=mesh, in_specs=in_specs, out_specs=out_specs, check_vma=False)
```

profile of v0, /device:TPU:6, one launch (start us, length us, event | category | flops | bytes accessed | tf_op | source)
XLA Modules:
  0.0 650.9 jit_solution(6691471587485620089)
XLA Ops:
  7.2 0.0 copy-start
  7.2 0.0 all-reduce.4.cloned.1.call-start
  7.2 21.8 %all_gather.3 = bf16[256,1024]{0,1:T(8,128)(2,1)S(1)} all-gather(bf16[256,64]{0,1:T(8,128)(2,1)} %param.5), channel_id=1, replica_groups=mesh['rows'=16,'sub'=16] {'sub'}, dimensions={1}, use_global_device_ids=true | all-gather | bytes 557056 | tf_op jit(solution)/shard_map/all_gather | solution.py:58
  29.0 5.3 fusion.14
  34.3 0.0 copy-done
  34.3 2.7 convolution_bitcast_fusion
  36.9 0.0 copy-start.2
  36.9 0.0 all-reduce.4.cloned.1.call-update
  37.0 0.0 all-reduce.6.cloned.1.call-start
  37.0 0.8 copy-done.2
  37.8 3.4 convert_reduce_fusion
  41.2 264.1 %all-reduce.4.cloned.1.call-done = f32[1024,1024]{0,1:T(8,128)} async-done(((f32[1024,1024]{0,1:T(8,128)}), f32[1024,1024]{0,1:T(8,128)}) %all-reduce.4.cloned.1.call-update) | async-done | bytes 4194320 | tf_op jit(solution)/shard_map/psum | solution.py:63
  305.3 3.9 multiply_reduce_fusion
  309.9 7.8 %fusion.28 = f32[1024,1024]{1,0:T(8,128)} fusion(f32[1024,1024]{0,1:T(8,128)} %all-reduce.4.cloned.1.call-done, f32[]{:T(128)S(6)} %add.47), kind=kOutput, calls=%fused_computation.30 | convolution fusion | flops 2149580800 | bytes 8388612 | tf_op jit(solution)/shard_map/dot_general | solution.py:41
  317.7 13.9 %multiply_add_fusion.2 = f32[1024,1024]{0,1:T(8,128)} fusion(f32[1024,1024]{0,1:T(8,128)} %all-reduce.4.cloned.1.call-done, f32[]{:T(128)S(6)} %add.47, f32[1024,1024]{1,0:T(8,128)} %fusion.28), kind=kOutput, calls=%fused_computation.12 | convolution fusion | flops 4305453056 | bytes 12582916 | tf_op jit(solution)/shard_map/dot_general | solution.py:41
  331.6 7.8 %fusion.21 = f32[1024,1024]{1,0:T(8,128)} fusion(f32[1024,1024]{0,1:T(8,128)} %multiply_add_fusion.2), kind=kOutput, calls=%fused_computation.28 | convolution fusion | flops 2148532224 | bytes 8388608 | tf_op jit(solution)/shard_map/dot_general | solution.py:41
  339.4 13.7 %multiply_add_fusion.1 = f32[1024,1024]{0,1:T(8,128)} fusion(f32[1024,1024]{0,1:T(8,128)} %multiply_add_fusion.2, f32[1024,1024]{1,0:T(8,128)} %fusion.21), kind=kOutput, calls=%fused_computation.10 | convolution fusion | flops 4303355904 | bytes 12582912 | tf_op jit(solution)/shard_map/dot_general | solution.py:41
  353.1 8.0 %fusion.18 = f32[1024,1024]{1,0:T(8,128)} fusion(f32[1024,1024]{0,1:T(8,128)} %multiply_add_fusion.1), kind=kOutput, calls=%fused_computation.25 | convolution fusion | flops 2148532224 | bytes 8388608 | tf_op jit(solution)/shard_map/dot_general | solution.py:41
  361.2 13.9 %multiply_add_fusion = f32[1024,1024]{0,1:T(8,128)} fusion(f32[1024,1024]{0,1:T(8,128)} %multiply_add_fusion.1, f32[1024,1024]{1,0:T(8,128)} %fusion.18), kind=kOutput, calls=%fused_computation.8 | convolution fusion | flops 4303355904 | bytes 12582912 | tf_op jit(solution)/shard_map/dot_general | solution.py:41
  375.1 2.9 fusion.11
  378.0 0.0 copy-start.1
  378.0 5.1 fusion.1
  383.1 0.0 all-reduce.6.cloned.1.call-update
  383.1 1.2 constant_dynamic-slice_fusion
  384.4 0.9 copy.9
  385.3 1.0 copy.10
  386.3 255.6 %all-reduce.6.cloned.1.call-done = (f32[256,1024]{0,1:T(8,128)}, f32[256,64]{0,1:T(8,128)}) async-done(((f32[256,1024]{0,1:T(8,128)}, f32[256,64]{0,1:T(8,128)}), (f32[256,1024]{0,1:T(8,128)}, f32[256,64]{0,1:T(8,128)})) %all-reduce.6.cloned.1.call-update) | async-done | bytes 1114128 | tf_op jit(solution)/shard_map/psum | solution.py:73
  641.9 0.7 dynamic-slice_add_fusion
  642.6 0.0 copy-done.1
  642.6 1.5 bitcast_divide_fusion
Async XLA Ops:
  7.2 27.1 %copy-start = (bf16[256,1024]{1,0:T(8,128)(2,1)S(1)}, bf16[256,1024]{1,0:T(8,128)(2,1)}, u32[]{:S(2)}) copy-start(bf16[256,1024]{1,0:T(8,128)(2,1)} %param.3) | copy-start | bytes 1572868
  7.2 298.1 %all-reduce.4.cloned.1.call-start = ((), (), s32[]{:S(2)}) async-start(), calls=%async_computation | async-start | bytes 8388608 | tf_op jit(solution)/shard_map/psum | solution.py:63
  36.9 0.8 copy-start.2
  37.0 604.9 %all-reduce.6.cloned.1.call-start = ((), (), s32[]{:S(2)}) async-start(), calls=%async_computation.1 | async-start | bytes 2228224 | tf_op jit(solution)/shard_map/psum | solution.py:73
  378.0 264.6 %copy-start.1 = (bf16[256,64]{0,1:T(8,128)(2,1)S(1)}, bf16[256,64]{0,1:T(8,128)(2,1)}, u32[]{:S(2)}) copy-start(bf16[256,64]{0,1:T(8,128)(2,1)} %param.5) | copy-start | bytes 98308
Sparse Core Ops, SparseCore 0:
  37.1 268.1 all-reduce.3
  383.3 258.5 all-reduce.5
where the time goes:
time: 652 us; the launch traced here: 651 us
  waiting for transfers between devices  520 us (80%)
  matrix products  81.1 us (12%)
  blocking collectives  21.8 us (3%)
  between operations  14.8 us (2%)
  other arithmetic  9.48 us (1%)
    psum x1, waiting for transfers between devices, body(): cross = lax.psum(partial, ('rows', 'sub'))  264 us
    psum x1, waiting for transfers between devices, body(): code_sums = lax.psum(code_sums, ('rows', 'sub'))  256 us
    dot_general x6, matrix products, bdot(): lax.dot_general(left.astype(jnp.bfloat16), right.astype(jnp.bfloat16), (d...  65.2 us
    all_gather x1, blocking collectives, body(): table = lax.all_gather(codebook, 'sub', axis=1, tiled=True)  21.8 us
  transfers between devices with their start and end apart: 2, of which 2 were waited for; matrix products, arithmetic and copies ran while one was open for 1% of the time, Pallas kernels for 0%

commit v1 on v0

--- a/solution.py
+++ b/solution.py
@@ -9,6 +9,27 @@
 coef_b = -4.775
 coef_c = 2.0315
 frob_eps = 1e-07
+
+
+def gather_around(shard, axis, dim):
+    peers, mine, rows = (lax.axis_size(axis), lax.axis_index(axis), shard.shape[dim])
+    right = [(i, (i + 1) % peers) for i in range(peers)]
+    left = [(i, (i - 1) % peers) for i in range(peers)]
+    out = jnp.zeros((*shard.shape[:dim], peers * rows, *shard.shape[dim + 1 :]), shard.dtype)
+    out = lax.dynamic_update_slice_in_dim(out, shard, mine * rows, axis=dim)
+    from_left = from_right = shard
+    middle = peers // 2
+    for turn in range(1, middle + 1):
+        from_left = lax.ppermute(from_left, axis, right)
+        out = lax.dynamic_update_slice_in_dim(
+            out, from_left, (mine - turn) % peers * rows, axis=dim
+        )
+        if turn < peers - middle:
+            from_right = lax.ppermute(from_right, axis, left)
+            out = lax.dynamic_update_slice_in_dim(
+                out, from_right, (mine + turn) % peers * rows, axis=dim
+            )
+    return out
 
 
 def one_hot_codes(code_block, count_codes):
@@ -55,7 +76,7 @@
 
 
 def body(embeddings, codes, codebook):
-    table = lax.all_gather(codebook, "sub", axis=1, tiled=True)
+    table = gather_around(codebook, "sub", 1)
     decoded = decode_rows(codes, table)
     partial = lax.dot_general(
         embeddings, decoded, (((0,), (0,)), ((), ())), preferred_element_type=jnp.float32

time: 652 us -> 671 us (1.029)
  starting transfers between devices: 0.08 us -> 23 us
  blocking collectives: 21.8 us -> 0 us
  waiting for transfers between devices: 520 us -> 537 us
    ppermute x0 -> x15, starting transfers between devices: none -> 23 us  [the longest x7 22.9 us: gather_around(): from_right = lax.ppermute(from_right, axis, left)]
    all_gather x1 -> x0, blocking collectives: 21.8 us -> none  [body(): table = lax.all_gather(codebook, 'sub', axis=1, tiled=True)]
    ppermute x0 -> x15, waiting for transfers between devices: none -> 15.1 us  [the longest x8 14.8 us: gather_around(): from_left = lax.ppermute(from_left, axis, right)]
  transfers between devices with their start and end apart: 2 -> 17, of which waited for: 2 -> 11; matrix products, arithmetic and copies ran while one was open for 1% -> 1% of each run, Pallas kernels for 0% -> 0%
where the time goes in v1:
time: 671 us; the launch traced here: 670 us
  waiting for transfers between devices  537 us (80%)
  matrix products  81.1 us (12%)
  starting transfers between devices  23 us (3%)
  between operations  14.8 us (2%)
  other arithmetic  9.48 us (1%)
    psum x1, waiting for transfers between devices, body(): cross = lax.psum(partial, ('rows', 'sub'))  267 us
    psum x1, waiting for transfers between devices, body(): code_sums = lax.psum(code_sums, ('rows', 'sub'))  255 us
    dot_general x6, matrix products, bdot(): lax.dot_general(left.astype(jnp.bfloat16), right.astype(jnp.bfloat16), (d...  65.1 us
    ppermute x7, starting transfers between devices, gather_around(): from_right = lax.ppermute(from_right, axis, left)  22.9 us
    ppermute x8, waiting for transfers between devices, gather_around(): from_left = lax.ppermute(from_left, axis, right)  14.8 us
  transfers between devices with their start and end apart: 17, of which 11 were waited for; matrix products, arithmetic and copies ran while one was open for 1% of the time, Pallas kernels for 0%

profile of v1, /device:TPU:6, one launch (start us, length us, event | category | flops | bytes accessed | tf_op | source)
XLA Modules:
  0.0 670.4 jit_solution(8375686706223122576)
XLA Ops:
  7.2 0.0 copy-start
  7.2 0.0 all-reduce.4.cloned.1.call-start
  7.2 0.0 collective-permute-start
  7.3 5.3 collective-permute-start.1
  12.6 0.8 constant_dynamic-update-slice_fusion.15
  13.4 1.0 collective-permute-done
  14.3 0.0 collective-permute-start.2
  14.3 0.1 collective-permute-done.1
  14.5 2.8 collective-permute-start.3
  17.3 1.6 collective-permute-done.2
  18.9 0.0 collective-permute-start.4
  18.9 0.0 collective-permute-done.3
  18.9 3.0 collective-permute-start.5
  21.9 1.6 collective-permute-done.4
  23.4 0.0 collective-permute-start.6
  23.5 0.0 collective-permute-done.5
  23.5 3.0 collective-permute-start.7
  26.4 1.6 collective-permute-done.6
  28.0 0.0 collective-permute-start.8
  28.0 0.0 collective-permute-done.7
  28.0 3.0 collective-permute-start.9
  31.0 1.6 collective-permute-done.8
  32.6 0.0 collective-permute-start.10
  32.6 0.0 collective-permute-done.9
  32.6 3.0 collective-permute-start.11
  35.5 1.6 collective-permute-done.10
  37.1 0.0 collective-permute-start.12
  37.1 0.0 collective-permute-done.11
  37.1 3.0 collective-permute-start.13
  40.1 1.6 collective-permute-done.12
  41.7 0.0 collective-permute-start.14
  41.7 0.0 collective-permute-done.13
  41.7 4.5 collective-permute-done.14
  46.2 5.3 fusion.14
  51.5 0.0 copy-done
  51.5 2.7 convolution_bitcast_fusion
  54.1 0.0 copy-start.2
  54.2 0.0 all-reduce.4.cloned.1.call-update
  54.2 0.0 all-reduce.6.cloned.1.call-start
  54.2 0.8 copy-done.2
  55.0 3.4 convert_reduce_fusion
  58.4 266.6 %all-reduce.4.cloned.1.call-done = f32[1024,1024]{0,1:T(8,128)} async-done(((f32[1024,1024]{0,1:T(8,128)}), f32[1024,1024]{0,1:T(8,128)}) %all-reduce.4.cloned.1.call-update) | async-done | bytes 4194320 | tf_op jit(solution)/shard_map/psum | solution.py:84
  325.0 3.9 multiply_reduce_fusion
  329.6 7.8 %fusion.28 = f32[1024,1024]{1,0:T(8,128)} fusion(f32[1024,1024]{0,1:T(8,128)} %all-reduce.4.cloned.1.call-done, f32[]{:T(128)S(6)} %add.206), kind=kOutput, calls=%fused_computation.30 | convolution fusion | flops 2149580800 | bytes 8388612 | tf_op jit(solution)/shard_map/dot_general | solution.py:62
  337.4 13.9 %multiply_add_fusion.2 = f32[1024,1024]{0,1:T(8,128)} fusion(f32[1024,1024]{0,1:T(8,128)} %all-reduce.4.cloned.1.call-done, f32[]{:T(128)S(6)} %add.206, f32[1024,1024]{1,0:T(8,128)} %fusion.28), kind=kOutput, calls=%fused_computation.12 | convolution fusion | flops 4305453056 | bytes 12582916 | tf_op jit(solution)/shard_map/dot_general | solution.py:62
  351.3 7.8 %fusion.21 = f32[1024,1024]{1,0:T(8,128)} fusion(f32[1024,1024]{0,1:T(8,128)} %multiply_add_fusion.2), kind=kOutput, calls=%fused_computation.28 | convolution fusion | flops 2148532224 | bytes 8388608 | tf_op jit(solution)/shard_map/dot_general | solution.py:62
  359.1 13.6 %multiply_add_fusion.1 = f32[1024,1024]{0,1:T(8,128)} fusion(f32[1024,1024]{0,1:T(8,128)} %multiply_add_fusion.2, f32[1024,1024]{1,0:T(8,128)} %fusion.21), kind=kOutput, calls=%fused_computation.10 | convolution fusion | flops 4303355904 | bytes 12582912 | tf_op jit(solution)/shard_map/dot_general | solution.py:62
  372.7 8.1 %fusion.18 = f32[1024,1024]{1,0:T(8,128)} fusion(f32[1024,1024]{0,1:T(8,128)} %multiply_add_fusion.1), kind=kOutput, calls=%fused_computation.25 | convolution fusion | flops 2148532224 | bytes 8388608 | tf_op jit(solution)/shard_map/dot_general | solution.py:62
  380.8 13.9 %multiply_add_fusion = f32[1024,1024]{0,1:T(8,128)} fusion(f32[1024,1024]{0,1:T(8,128)} %multiply_add_fusion.1, f32[1024,1024]{1,0:T(8,128)} %fusion.18), kind=kOutput, calls=%fused_computation.8 | convolution fusion | flops 4303355904 | bytes 12582912 | tf_op jit(solution)/shard_map/dot_general | solution.py:62
  394.7 2.9 fusion.11
  397.6 0.0 copy-start.1
  397.6 5.1 fusion.1
  402.8 0.0 all-reduce.6.cloned.1.call-update
  402.8 1.0 copy.10
  403.8 1.2 constant_dynamic-slice_fusion.1
  405.0 0.9 copy.9
  405.9 255.5 %all-reduce.6.cloned.1.call-done = (f32[256,1024]{0,1:T(8,128)}, f32[256,64]{0,1:T(8,128)}) async-done(((f32[256,1024]{0,1:T(8,128)}, f32[256,64]{0,1:T(8,128)}), (f32[256,1024]{0,1:T(8,128)}, f32[256,64]{0,1:T(8,128)})) %all-reduce.6.cloned.1.call-update) | async-done | bytes 1114128 | tf_op jit(solution)/shard_map/psum | solution.py:94
  661.4 0.7 fusion.30
  662.1 0.0 copy-done.1
  662.1 1.5 bitcast_divide_fusion
  (16 shorter events, 0.1 us)
Async XLA Ops:
  7.2 44.3 %copy-start = (bf16[256,1024]{1,0:T(8,128)(2,1)S(1)}, bf16[256,1024]{1,0:T(8,128)(2,1)}, u32[]{:S(2)}) copy-start(bf16[256,1024]{1,0:T(8,128)(2,1)} %param.3) | copy-start | bytes 1572868
  7.2 317.8 %all-reduce.4.cloned.1.call-start = ((), (), s32[]{:S(2)}) async-start(), calls=%async_computation | async-start | bytes 8388608 | tf_op jit(solution)/shard_map/psum | solution.py:84
  7.2 7.1 %collective-permute-start = (bf16[256,64]{0,1:T(8,128)(2,1)}, bf16[256,64]{0,1:T(8,128)(2,1)S(1)}, u32[]{:S(2)}, u32[]{:S(2)}) collective-permute-start(bf16[256,64]{0,1:T(8,128)(2,1)} %param.5), channel_id=1, source_target_pairs={{0,1},{1,2},{2,3},{3,4},{4,5},{5,6},{6,7},{7,8},{8,9},{9,10},{10,1... | collective-permute-start | bytes 98312 | tf_op jit(solution)/shard_map/ppermute | solution.py:23
  7.3 7.2 %collective-permute-start.1 = (bf16[256,64]{0,1:T(8,128)(2,1)}, bf16[256,64]{0,1:T(8,128)(2,1)S(1)}, u32[]{:S(2)}, u32[]{:S(2)}) collective-permute-start(bf16[256,64]{0,1:T(8,128)(2,1)} %param.5), channel_id=1, source_target_pairs={{0,15},{1,0},{2,1},{3,2},{4,3},{5,4},{6,5},{7,6},{8,7},{9,8},{10,9... | collective-permute-start | bytes 98312 | tf_op jit(solution)/shard_map/ppermute | solution.py:28
  14.3 4.6 collective-permute-start.2
  14.5 4.4 collective-permute-start.3
  18.9 4.6 collective-permute-start.4
  18.9 4.6 collective-permute-start.5
  23.4 4.6 collective-permute-start.6
  23.5 4.6 collective-permute-start.7
  28.0 4.6 collective-permute-start.8
  28.0 4.6 collective-permute-start.9
  32.6 4.6 collective-permute-start.10
  32.6 4.6 collective-permute-start.11
  37.1 4.6 collective-permute-start.12
  37.1 4.6 collective-permute-start.13
  41.7 4.6 collective-permute-start.14
  54.1 0.8 copy-start.2
  54.2 607.2 %all-reduce.6.cloned.1.call-start = ((), (), s32[]{:S(2)}) async-start(), calls=%async_computation.1 | async-start | bytes 2228224 | tf_op jit(solution)/shard_map/psum | solution.py:94
  397.6 264.5 %copy-start.1 = (bf16[256,64]{0,1:T(8,128)(2,1)S(1)}, bf16[256,64]{0,1:T(8,128)(2,1)}, u32[]{:S(2)}) copy-start(bf16[256,64]{0,1:T(8,128)(2,1)} %param.5) | copy-start | bytes 98308
Sparse Core Ops, SparseCore 0:
  54.3 270.6 all-reduce.3
  402.9 258.4 all-reduce.5
